TPU v7x, 32 devices: a whole 2x2x4 slice. The times are simulated.
32 devices in a mesh: groups: 2 (over x), ctx: 8 (over z, y), heads: 2 (over core).
Axes of the slice: x: 2, y: 2, z: 4, core: 2. Of those that a mesh axis runs over, the one named last changes fastest.
Arguments:
- ssm_input: bfloat16 [4, 2048, 8192], P('groups', 'ctx', 'heads'), parts along dimension 0, may hold values from -6 to 6
- b_proj: bfloat16 [4, 2048, 512], P('groups', 'ctx', 'heads'), parts along dimension 0, may hold values from -600 to 600
- c_proj: bfloat16 [4, 2048, 512], P('groups', 'ctx', 'heads'), parts along dimension 0, may hold values from -6 to 6
- step_size: float32 [4, 128, 2048], P('groups', 'heads', 'ctx'), parts along dimension 0, may hold values from 0.01 to 0.04
- log_decay: float32 [4, 128, 2048], P('groups', 'heads', 'ctx'), parts along dimension 0, may hold values from -1 to 0
- skip_gain: float32 [128], P('heads'), may hold values from 0.5 to 1.5
- request_of_slot: int32 [16], P(('groups', 'ctx')), parts along dimension 0, may hold values from 0 to 1, as said below
- new_input: bfloat16 [16, 4, 8192], P(('groups', 'ctx'), None, 'heads'), parts along dimension 0, may hold values from -6 to 6
- new_b: bfloat16 [16, 4, 512], P(('groups', 'ctx'), None, 'heads'), parts along dimension 0, may hold values from -0.5 to 0.5
- new_c: bfloat16 [16, 4, 512], P(('groups', 'ctx'), None, 'heads'), parts along dimension 0, may hold values from -6 to 6
- new_step: float32 [16, 4, 128], P(('groups', 'ctx'), None, 'heads'), parts along dimension 0, may hold values from 0.2 to 1
- new_log_decay: float32 [16, 4, 128], P(('groups', 'ctx'), None, 'heads'), parts along dimension 0, may hold values from -0.3 to -0.02
- out_weight: bfloat16 [8192, 8192], P('heads', 'ctx'), may hold values from -0.0625 to 0.0625
Outputs:
- prefill_out: bfloat16 [4, 2048, 8192], P('groups', 'ctx', 'heads'), parts along dimension 0
- decoded: bfloat16 [16, 4, 8192], P('groups', None, 'ctx'), parts along dimension 0
There are 2 independent parts, one for each index of `groups`. A program takes and returns all parts, laid end to end along the dimension named above; an argument that names none is the same for every part. Nothing has to cross between parts.
Inputs may be any that keep to these rules, and one draw needn't show every extreme that they name: `request_of_slot`: every prompt is named by at least one slot.
All inputs are finite; a program needn't handle non-finite values.
Results may differ from a plain program's by a relative error of at most 0.008.
Values may be sent and summed in bfloat16 or wider, within the bound.
No kernel may reach another device: no remote copies, remote signals or barrier semaphores. Data moves between devices by JAX's collectives and lax.ppermute only.
A program may use at most 320 MiB of HBM per device.

v0:
```python
import jax
import jax.numpy as jnp
from jax import lax
from jax.sharding import PartitionSpec as P

HEADS = 128
HEAD_DIM = 64
STATE = 128
GROUPS = 4
HIGH = lax.Precision.HIGHEST


def block_terms(block_input, block_b, block_c, block_step, block_logd):
    block_size = block_input.shape[0]
    head_count = block_step.shape[0]
    per_group = HEADS // GROUPS
    group_count = head_count // per_group
    cumulative = jnp.cumsum(block_logd, axis=1)
    block_total = cumulative[:, -1]
    inputs_head = block_input.reshape(block_size, group_count, per_group, HEAD_DIM)
    b_groups = block_b.reshape(block_size, group_count, STATE)
    c_groups = block_c.reshape(block_size, group_count, STATE)
    scores = jnp.einsum("tgn,sgn->gts", c_groups, b_groups, preferred_element_type=jnp.float32)
    row_index = lax.broadcasted_iota(jnp.int32, (block_size, block_size), 0)
    col_index = lax.broadcasted_iota(jnp.int32, (block_size, block_size), 1)
    causal = row_index >= col_index
    log_gap = cumulative[:, :, None] - cumulative[:, None, :]
    decay_rate = (
        jnp.where(causal, jnp.exp(jnp.where(causal, log_gap, 0.0)), 0.0) * block_step[:, None, :]
    )
    mixing = (
        scores[:, None, :, :] * decay_rate.reshape(group_count, per_group, block_size, block_size)
    ).astype(jnp.bfloat16)
    local_out = jnp.einsum(
        "gkts,sgkp->tgkp", mixing, inputs_head, preferred_element_type=jnp.float32
    )
    weighting = jnp.exp(block_total[:, None] - cumulative) * block_step
    weighted = (weighting.T.reshape(block_size, group_count, per_group, 1) * inputs_head).astype(
        jnp.bfloat16
    )
    block_state = jnp.einsum(
        "sgkp,sgn->gkpn", weighted, b_groups, preferred_element_type=jnp.float32
    )
    return (cumulative, block_total.reshape(group_count, per_group), local_out, block_state)


def finish(local_out, cumulative, block_c, entering, block_input, skip_gain):
    block_size = block_input.shape[0]
    group_count, per_group = (entering.shape[0], entering.shape[1])
    c_groups = block_c.reshape(block_size, group_count, STATE).astype(jnp.float32)
    carried = jnp.einsum("tgn,gkpn->tgkp", c_groups, entering, precision=HIGH)
    carried = carried * jnp.exp(cumulative).T.reshape(block_size, group_count, per_group, 1)
    inputs_head = block_input.reshape(block_size, group_count, per_group, HEAD_DIM)
    skipped = skip_gain.reshape(group_count, per_group, 1) * inputs_head
    return (
        (local_out + carried + skipped)
        .reshape(block_size, group_count * per_group * HEAD_DIM)
        .astype(jnp.bfloat16)
    )


def range_decay(all_totals, low, high):
    place = lax.broadcasted_iota(jnp.int32, all_totals.shape, 0)
    keep = (place >= low) & (place <= high)
    return jnp.exp(jnp.sum(jnp.where(keep, all_totals, 0.0), axis=0))


def scale(factor, state):
    return factor[..., None, None] * state


def send(value, pairs):
    return lax.ppermute(value.astype(jnp.bfloat16), "ctx", pairs).astype(jnp.float32)


def prefix_states(states, all_totals):
    count = lax.axis_size("ctx")
    columns = count // 2
    place = lax.axis_index("ctx")
    row = place % 2
    column = place // 2
    half = states.shape[-2] // 2
    first = states[..., :half, :]
    second = states[..., half:, :]
    row_zero = row == 0
    mine = jnp.where(row_zero, first, second)
    other = jnp.where(row_zero, second, first)
    across = [(2 * m, 2 * m + 1) for m in range(columns)] + [
        (2 * m + 1, 2 * m) for m in range(columns)
    ]
    received = send(other, across)
    even_state = jnp.where(row_zero, mine, received)
    odd_state = jnp.where(row_zero, received, mine)
    odd_decay = range_decay(all_totals, 2 * column + 1, 2 * column + 1)
    window = scale(odd_decay, even_state) + odd_state
    before = jnp.zeros_like(window)
    step = 1
    while step < columns:
        pairs = [(y + 2 * m, y + 2 * (m + step)) for y in range(2) for m in range(columns - step)]
        got = send(window, pairs)
        low = 2 * (column - step) + 2
        before = scale(range_decay(all_totals, low, 2 * column - 1), got) + before
        if 2 * step < columns:
            window = scale(range_decay(all_totals, low, 2 * column + 1), got) + window
        step *= 2
    even_decay = range_decay(all_totals, 2 * column, 2 * column)
    odd_entering = scale(even_decay, before) + even_state
    outgoing = jnp.where(row_zero, odd_entering, before)
    partner = send(outgoing, across)
    own_half = jnp.where(row_zero, before, odd_entering)
    first_half = jnp.where(row_zero, own_half, partner)
    second_half = jnp.where(row_zero, partner, own_half)
    return jnp.concatenate([first_half, second_half], axis=-2)


def shards(
    ssm_input,
    b_proj,
    c_proj,
    step_size,
    log_decay,
    skip_gain,
    request_of_slot,
    new_input,
    new_b,
    new_c,
    new_step,
    new_log_decay,
    out_weight,
):
    request_count = ssm_input.shape[0]
    count = lax.axis_size("ctx")
    place = lax.axis_index("ctx")
    terms = []
    for request in range(request_count):
        terms.append(
            block_terms(
                ssm_input[request],
                b_proj[request],
                c_proj[request],
                step_size[request],
                log_decay[request],
            )
        )
    totals = jnp.stack([term[1] for term in terms])
    states = jnp.stack([term[3] for term in terms])
    group_count, per_group = (totals.shape[1], totals.shape[2])
    slots, steps = (new_input.shape[0], new_input.shape[1])
    pieces = [
        totals,
        request_of_slot.astype(jnp.float32),
        new_input.astype(jnp.float32),
        new_b.astype(jnp.float32),
        new_c.astype(jnp.float32),
        new_step,
        new_log_decay,
    ]
    packed = jnp.concatenate([piece.reshape(-1) for piece in pieces])
    gathered = lax.all_gather(packed, "ctx")
    unpacked = []
    offset = 0
    for piece in pieces:
        size = piece.size
        unpacked.append(gathered[:, offset : offset + size].reshape((count,) + piece.shape))
        offset += size
    all_totals, all_request, all_input, all_b, all_c, all_step, all_logd = unpacked
    all_slots = count * slots
    all_request = all_request.reshape(all_slots)
    all_input = all_input.reshape(all_slots, steps, group_count, per_group, HEAD_DIM)
    all_b = all_b.reshape(all_slots, steps, group_count, STATE)
    all_c = all_c.reshape(all_slots, steps, group_count, STATE)
    all_step = all_step.reshape(all_slots, steps, group_count, per_group)
    all_logd = all_logd.reshape(all_slots, steps, group_count, per_group)
    later = range_decay(all_totals, place + 1, count - 1)
    weighted_states = scale(later, states)
    projected = jnp.einsum("rgkpn,jugn->rjugkp", weighted_states, all_c, precision=HIGH)
    request_numbers = lax.broadcasted_iota(jnp.int32, (request_count, 1), 0).astype(jnp.float32)
    chosen = (request_numbers == all_request[None, :]).astype(jnp.float32)
    contribution = jnp.einsum("rj,rjugkp->jugkp", chosen, projected, precision=HIGH)
    from_prompt = lax.psum(contribution, "ctx")
    cum_logd = jnp.cumsum(all_logd, axis=1)
    inner = jnp.einsum("jvgn,jugn->jvug", all_b, all_c, precision=HIGH)
    driven = all_step[..., None] * all_input
    outputs = []
    for u in range(steps):
        value = jnp.exp(cum_logd[:, u])[..., None] * from_prompt[:, u]
        for v in range(u + 1):
            gap = jnp.exp(cum_logd[:, u] - cum_logd[:, v])
            coefficient = gap * inner[:, v, u][:, :, None]
            value = value + coefficient[..., None] * driven[:, v]
        value = value + skip_gain.reshape(group_count, per_group, 1) * all_input[:, u]
        outputs.append(value.reshape(all_slots, -1).astype(jnp.bfloat16))
    new_output = jnp.stack(outputs, axis=1)
    partial_value = jnp.einsum(
        "jup,pd->jud", new_output, out_weight, preferred_element_type=jnp.float32
    )
    decoded = lax.psum(partial_value, "heads").astype(jnp.bfloat16)
    entering = prefix_states(states, all_totals)
    prefill_rows = []
    for request in range(request_count):
        prefill_rows.append(
            finish(
                terms[request][2],
                terms[request][0],
                c_proj[request],
                entering[request],
                ssm_input[request],
                skip_gain,
            )
        )
    prefill_out = jnp.stack(prefill_rows)
    return (prefill_out, decoded)


def solution(mesh):
    in_specs = (
        P("groups", "ctx", "heads"),
        P("groups", "ctx", "heads"),
        P("groups", "ctx", "heads"),
        P("groups", "heads", "ctx"),
        P("groups", "heads", "ctx"),
        P("heads"),
        P(("groups", "ctx")),
        P(("groups", "ctx"), None, "heads"),
        P(("groups", "ctx"), None, "heads"),
        P(("groups", "ctx"), None, "heads"),
        P(("groups", "ctx"), None, "heads"),
        P(("groups", "ctx"), None, "heads"),
        P("heads", "ctx"),
    )
    out_specs = (P("groups", "ctx", "heads"), P("groups", None, "ctx"))
    return jax.shard_map(shards, mesh=mesh, in_specs=in_specs, out_specs=out_specs, check_vma=False)
```

profile of v0, /device:TPU:26, one launch (start us, length us, event | category | flops | bytes accessed | tf_op | source)
XLA Modules:
  0.0 315.2 jit_solution(35564834466314363)
XLA Ops:
  19.5 3.9 %fusion.76 = (bf16[1,256,4096]{2,1,0:T(8,128)(2,1)}, bf16[1,256,4096]{2,1,0:T(8,128)(2,1)S(1)}) fusion(bf16[2,256,4096]{2,1,0:T(8,128)(2,1)} %param.13), kind=kLoop, calls=%fused_computation.144 | loop fusion | bytes 8388608 | tf_op jit(solution)/shard_map/slice | solution.py:138
  23.4 4.2 %copy.105 = bf16[1,256,4096]{1,2,0:T(8,128)(2,1)} copy(bf16[1,256,4096]{2,1,0:T(8,128)(2,1)} %get-tuple-element.18) | data formatting | bytes 4194304 | tf_op jit(solution)/shard_map/slice | solution.py:138
  27.7 2.5 copy.110
  30.4 2.5 fusion.52
  33.6 1.7 select_convert_fusion.1
  39.5 1.6 fusion.82
  45.4 8.0 %fusion = f32[2,32,256,64]{2,3,1,0:T(8,128)} fusion(bf16[256,2,32,64]{0,3,2,1:T(8,128)(2,1)} %bitcast.245, f32[2,32,256]{2,1,0:T(8,128)} %bitcast.270, f32[2,32,256]{2,1,0:T(8,128)} %reduce_window_sum.59, f32[2,256,256]{2,1,0:T(8,128)S(1)} %fusion.88, pred[256,256]{1,0:T(8,128)(4,1)} %iota_compare_fusion), kind=kOutput, calls=%fused_computation.2 | convolution fusion | flops 562036736 | bytes 7012352 | tf_op jit(solution)/shard_map/gkts,sgkp->tgkp/dot_general | solution.py:34
  53.4 6.6 %fusion.1 = f32[2,32,256,64]{2,3,1,0:T(8,128)} fusion(bf16[256,2,32,64]{0,3,2,1:T(8,128)(2,1)S(1)} %bitcast.248, f32[2,32,256]{2,1,0:T(8,128)S(1)} %bitcast.269, f32[2,32,256]{2,1,0:T(8,128)S(1)} %copy-done.32, f32[2,256,256]{2,1,0:T(8,128)S(1)} %fusion.89, pred[256,256]{1,0:T(8,128)(4,1)S(1)} %copy-done.31), kind=kOutput, calls=%fused_computation.3 | convolution fusion | flops 562036736 | bytes 7012352 | tf_op jit(solution)/shard_map/gkts,sgkp->tgkp/dot_general | solution.py:34
  62.5 30.0 %all-reduce.7.cloned.1.call-done = f32[152584]{0:T(1024)} async-done(((f32[152584]{0:T(1024)}), f32[152584]{0:T(1024)}) %all-reduce.7.cloned.1.call-update) | async-done | bytes 610352
  92.5 2.3 reshape.861
  100.3 2.0 slice.261
  103.2 1.7 mul.677
  105.8 1.7 mul.693
  108.4 1.7 mul.699
  113.2 12.9 %fusion.49 = f32[2,8,4,2,32,64]{5,1,4,0,2,3:T(8,128)S(1)} fusion(f32[8,4,2,128,1,1]{3,0,2,1,5,4:T(8,128)S(1)} %bitcast.262, f32[1,2,32,64,128]{4,3,2,1,0:T(8,128)} %copy-done, f32[1,2,32,64,128]{4,3,2,1,0:T(8,128)S(1)} %fusion.52, f32[2,2,32]{2,1,0:T(2,128)S(1)} %exp.239), kind=kOutput, calls=%fused_computation.71 | convolution fusion | flops 404750336 | bytes 5276160 | tf_op jit(solution)/shard_map/rgkpn,jugn->rjugkp/dot_general | solution.py:176
  126.1 4.9 %fusion.47 = f32[8,1,4,2,32,64]{5,1,4,3,2,0:T(1,128)S(1)} fusion(pred[2,8,1,1,1,1]{0,2,5,4,3,1:T(4,128)(4,1)S(1)} %copy.162, f32[2,8,4,2,32,64]{5,1,4,0,2,3:T(8,128)S(1)} %fusion.49), kind=kOutput, calls=%fused_computation.69 | convolution fusion | flops 3145728 | bytes 1572880 | tf_op jit(solution)/shard_map/rj,rjugkp->jugkp/dot_general | solution.py:179
  132.1 2.5 reshape_reshape.15
  134.7 3.9 %fusion.58 = (bf16[2,2,32,32,128]{4,3,2,1,0:T(8,128)(2,1)}, f32[2,2,32,32,128]{4,3,2,1,0:T(8,128)}) fusion(bf16[2,2,32,32,128]{4,3,2,1,0:T(8,128)(2,1)S(1)} %collective-permute-done, pred[]{:T(512)S(6)} %eq.20, f32[2,2,32]{2,1,0:T(2,128)S(1)} %exp.226, f32[1,2,32,64,128]{4,3,2,1,0:T(8,128)} %copy-done, f32[1,2,32,64,128]{4,3,2,1,0:T(8,128)S(1)} %fusion.52), kind=kLoop, calls=%fused_computation.77 | loop fusion | flops 4718592 | bytes 8389121 | tf_op jit(solution)/shard_map/convert_element_type | solution.py:73
  142.3 1.7 squeeze.40
  156.7 1.9 mul.749
  158.6 1.7 squeeze.43
  160.3 1.7 squeeze.46
  162.0 1.5 mul.702
  163.6 1.7 mul.703
  166.8 1.7 mul.725
  168.5 1.7 copy.211
  170.2 1.7 squeeze.44
  171.9 1.7 copy.210
  173.6 1.7 squeeze.47
  185.1 3.0 fusion.30
  189.4 53.2 %all-reduce.5.cloned.1.call-done = f32[8,4,2,32,64]{4,3,2,0,1:T(8,128)} async-done(((f32[8,4,2,32,64]{4,3,2,0,1:T(8,128)}), f32[8,4,2,32,64]{4,3,2,0,1:T(8,128)}) %all-reduce.5.cloned.1.call-update) | async-done | bytes 524304 | tf_op jit(solution)/shard_map/psum | solution.py:180
  242.6 2.2 fusion.77
  244.8 1.7 squeeze.36
  246.6 1.7 squeeze.39
  248.3 1.7 squeeze.42
  250.0 1.7 squeeze.45
  251.7 1.7 add_convert_fusion.1
  253.6 3.1 select_convert_fusion
  256.6 7.5 %collective-permute-start.3 = (bf16[2,2,32,32,128]{4,3,2,1,0:T(8,128)(2,1)}, bf16[2,2,32,32,128]{4,3,2,1,0:T(8,128)(2,1)}, u32[]{:S(2)}, u32[]{:S(2)}) collective-permute-start(bf16[2,2,32,32,128]{4,3,2,1,0:T(8,128)(2,1)} %select_convert_fusion), channel_id=1, source_target_pairs={{0,2},{4,6},{8,10},{12,14},{2,0},{6,4},{10,8},{14,12},{1,3},{5,7},... | collective-permute-start | bytes 3145736 | tf_op jit(solution)/shard_map/ppermute | solution.py:73
  264.4 4.9 %fusion.2 = f32[8,4,1024]{2,0,1:T(8,128)S(1)} fusion(bf16[4096,1024]{1,0:T(8,128)(2,1)} %param.25, bf16[8,1,4096]{2,0,1:T(8,128)(2,1)S(1)} %get-tuple-element.37, bf16[8,1,4096]{2,0,1:T(8,128)(2,1)S(1)} %get-tuple-element.36, bf16[8,1,4096]{2,0,1:T(8,128)(2,1)S(1)} %get-tuple-element.43, bf16[8,1,4096]{2,0,1:T(8,128)(2,1)S(1)} %get-tuple-element.42), kind=kOutput, calls=%fused_computation.4 | convolution fusion | flops 268828672 | bytes 8781824 | tf_op jit(solution)/shard_map/jup,pd->jud/dot_general | solution.py:194
  269.2 4.4 %all-reduce.8 = bf16[8,4,1024]{2,0,1:T(8,128)(2,1)} all-reduce(f32[8,4,1024]{2,0,1:T(8,128)S(1)} %fusion.2), channel_id=1, replica_groups=mesh['groups'=2,'ctx'=8,'heads'=2] {'heads'}, use_global_device_ids=true, to_apply=%region_12.13 | all-reduce | flops 32768 | bytes 196608 | tf_op jit(solution)/shard_map/psum | solution.py:197
  275.1 6.9 %collective-permute-done.3 = bf16[2,2,32,32,128]{4,3,2,1,0:T(8,128)(2,1)} collective-permute-done((bf16[2,2,32,32,128]{4,3,2,1,0:T(8,128)(2,1)}, bf16[2,2,32,32,128]{4,3,2,1,0:T(8,128)(2,1)}, u32[]{:S(2)}, u32[]{:S(2)}) %collective-permute-start.3) | collective-permute-done | bytes 1048608 | tf_op jit(solution)/shard_map/ppermute | solution.py:73
  282.0 2.8 convert_select_fusion.1
  285.2 4.0 %fusion.18 = bf16[256,2,32,64]{0,3,2,1:T(8,128)(2,1)} fusion(bf16[256,2,32,64]{0,3,2,1:T(8,128)(2,1)S(1)} %bitcast.246, f32[2,32,256,64]{2,3,1,0:T(8,128)S(1)} %copy-done.11, bf16[256,2,128,1]{0,2,3,1:T(8,128)(2,1)S(1)} %bitcast.256, f32[2,2,32,32,128]{4,3,2,1,0:T(8,128)S(1)} %get-tuple-element.16, f32[2,2,32,32,128]{4,3,2,1,0:T(8,128)S(1)} %get-tuple-element.17, ...), kind=kOutput, calls=%fused_computation.29 | convolution fusion | flops 1617428480 | bytes 12779776 | tf_op jit(solution)/shard_map/tgn,gkpn->tgkp/dot_general | solution.py:51
  289.2 4.4 %copy.119 = bf16[1,256,4096]{2,1,0:T(8,128)(2,1)} copy(bf16[1,256,4096]{1,2,0:T(8,128)(2,1)} %bitcast.251) | data formatting | bytes 4194304 | tf_op jit(solution)/shard_map/convert_element_type | solution.py:58
  293.5 6.6 %fusion.21 = bf16[256,2,32,64]{0,3,2,1:T(8,128)(2,1)} fusion(bf16[256,2,32,64]{0,3,2,1:T(8,128)(2,1)S(1)} %bitcast.249, f32[2,32,256,64]{2,3,1,0:T(8,128)} %fusion.1, bf16[256,2,128,1]{0,2,3,1:T(8,128)(2,1)S(1)} %bitcast.254, f32[2,2,32,32,128]{4,3,2,1,0:T(8,128)} %copy-done.7, f32[2,2,32,32,128]{4,3,2,1,0:T(8,128)} %copy-done.6, ...), kind=kOutput, calls=%fused_computation.32 | convolution fusion | flops 1617428480 | bytes 12779776 | tf_op jit(solution)/shard_map/tgn,gkpn->tgkp/dot_general | solution.py:51
  300.1 4.3 %copy.120 = bf16[1,256,4096]{2,1,0:T(8,128)(2,1)} copy(bf16[1,256,4096]{1,2,0:T(8,128)(2,1)} %bitcast.250) | data formatting | bytes 4194304 | tf_op jit(solution)/shard_map/convert_element_type | solution.py:58
  304.4 4.0 %pad_maximum_fusion.1 = bf16[2,256,4096]{2,1,0:T(8,128)(2,1)} fusion(bf16[1,256,4096]{2,1,0:T(8,128)(2,1)} %copy.120, bf16[1,256,4096]{2,1,0:T(8,128)(2,1)S(1)} %copy-done.10), kind=kLoop, calls=%fused_computation.37 | loop fusion | flops 2097152 | bytes 8388608 | tf_op jit(solution)/shard_map/stack | solution.py:211
  (246 shorter events, 65.9 us)
Async XLA Ops:
  7.2 11.5 %copy-start.24 = (f32[2,64,256]{2,1,0:T(8,128)S(1)}, f32[2,64,256]{2,1,0:T(8,128)}, u32[]{:S(2)}) copy-start(f32[2,64,256]{2,1,0:T(8,128)} %param.16) | copy-start | bytes 393220
  7.2 85.3 %all-reduce.7.cloned.1.call-start = ((), (), s32[]{:S(2)}) async-start(), calls=%async_computation.1 | async-start | bytes 1228800
  18.6 224.0 %all-reduce.5.cloned.1.call-start = ((), (), s32[]{:S(2)}) async-start(), calls=%async_computation | async-start | bytes 2097152 | tf_op jit(solution)/shard_map/psum | solution.py:180
  23.4 4.2 %copy-start.30 = (bf16[2,256,256]{2,1,0:T(8,128)(2,1)S(1)}, bf16[2,256,256]{2,1,0:T(8,128)(2,1)}, u32[]{:S(2)}) copy-start(bf16[2,256,256]{2,1,0:T(8,128)(2,1)} %param.14) | copy-start | bytes 786436
  33.6 3.2 %copy-start.25 = (f32[2,64,256]{2,1,0:T(8,128)S(1)}, f32[2,64,256]{2,1,0:T(8,128)}, u32[]{:S(2)}) copy-start(f32[2,64,256]{2,1,0:T(8,128)} %param.16) | copy-start | bytes 393220
  35.3 99.4 %collective-permute-start = (bf16[2,2,32,32,128]{4,3,2,1,0:T(8,128)(2,1)}, bf16[2,2,32,32,128]{4,3,2,1,0:T(8,128)(2,1)S(1)}, u32[]{:S(2)}, u32[]{:S(2)}) collective-permute-start(bf16[2,2,32,32,128]{4,3,2,1,0:T(8,128)(2,1)} %select_convert_fusion.1), channel_id=1, source_target_pairs={{0,2},{4,6},{8,10},{12,14},{2,0},{6,4},{10,8},{14,12},{1,3},{5,7},... | collective-permute-start | bytes 3145736 | tf_op jit(solution)/shard_map/ppermute | solution.py:73
  45.3 8.0 %copy-start.4 = (bf16[1,256,4096]{1,2,0:T(8,128)(2,1)S(1)}, bf16[1,256,4096]{1,2,0:T(8,128)(2,1)}, u32[]{:S(2)}) copy-start(bf16[1,256,4096]{1,2,0:T(8,128)(2,1)} %copy.110) | copy-start | bytes 6291460
  45.3 8.0 %copy-start.31 = (pred[256,256]{1,0:T(8,128)(4,1)S(1)}, pred[256,256]{1,0:T(8,128)(4,1)}, u32[]{:S(2)}) copy-start(pred[256,256]{1,0:T(8,128)(4,1)} %iota_compare_fusion) | copy-start | bytes 196612
  45.3 8.0 %copy-start.32 = (f32[2,32,256]{2,1,0:T(8,128)S(1)}, f32[2,32,256]{2,1,0:T(8,128)}, u32[]{:S(2)}) copy-start(f32[2,32,256]{2,1,0:T(8,128)} %reduce_window_sum.63) | copy-start | bytes 196612
  45.3 8.0 %copy-start.33 = (f32[1,64,256]{2,1,0:T(8,128)S(1)}, f32[1,64,256]{2,1,0:T(8,128)}, u32[]{:S(2)}) copy-start(f32[1,64,256]{2,1,0:T(8,128)} %get-tuple-element.45) | copy-start | bytes 196612
  53.4 6.6 %copy-start.50 = (f32[64]{0:T(128)S(1)}, f32[64]{0:T(128)}, u32[]{:S(2)}) copy-start(f32[64]{0:T(128)} %param.18) | copy-start | bytes 772
  60.1 32.4 %copy-start.48 = (f32[2,32]{1,0:T(2,128)}, f32[2,32]{1,0:T(2,128)S(1)}, u32[]{:S(2)}) copy-start(f32[2,32]{1,0:T(2,128)S(1)} %mul.656) | copy-start | bytes 772
  134.7 3.9 %copy-start.41 = (f32[2,2,32]{2,1,0:T(2,128)}, f32[2,2,32]{2,1,0:T(2,128)S(1)}, u32[]{:S(2)}) copy-start(f32[2,2,32]{2,1,0:T(2,128)S(1)} %exp.226) | copy-start | bytes 1540
  134.7 5.2 %copy-start.8 = (f32[8,4,2,32,64]{4,3,2,1,0:T(8,128)S(1)}, f32[8,4,2,32,64]{4,3,2,1,0:T(8,128)}, u32[]{:S(2)}) copy-start(f32[8,4,2,32,64]{4,3,2,1,0:T(8,128)} %reshape_reshape.15) | copy-start | bytes 1572868
  138.6 46.6 %collective-permute-start.1 = (bf16[2,2,32,32,128]{4,3,2,1,0:T(8,128)(2,1)}, bf16[2,2,32,32,128]{4,3,2,1,0:T(8,128)(2,1)}, u32[]{:S(2)}, u32[]{:S(2)}) collective-permute-start(bf16[2,2,32,32,128]{4,3,2,1,0:T(8,128)(2,1)} %get-tuple-element.14), channel_id=1, source_target_pairs={{0,4},{4,8},{8,12},{2,6},{6,10},{10,14},{1,5},{5,9},{9,13},{3,7},{... | collective-permute-start | bytes 3145736 | tf_op jit(solution)/shard_map/ppermute | solution.py:73
  140.2 7.0 %copy-start.9 = (f32[8,4,2,32,64]{4,3,2,1,0:T(8,128)S(1)}, f32[8,4,2,32,64]{4,3,2,1,0:T(8,128)}, u32[]{:S(2)}) copy-start(f32[8,4,2,32,64]{4,3,2,1,0:T(8,128)} %reshape_reshape.15) | copy-start | bytes 1572868
  146.5 3.3 %copy-start.40 = (f32[8,2,32]{2,1,0:T(2,128)S(1)}, f32[8,2,32]{2,1,0:T(2,128)}, u32[]{:S(2)}) copy-start(f32[8,2,32]{2,1,0:T(2,128)} %get-tuple-element.59) | copy-start | bytes 6148
  147.2 3.4 %copy-start.39 = (f32[8,2,32]{2,1,0:T(2,128)S(1)}, f32[8,2,32]{2,1,0:T(2,128)}, u32[]{:S(2)}) copy-start(f32[8,2,32]{2,1,0:T(2,128)} %get-tuple-element.60) | copy-start | bytes 6148
  148.2 3.4 %copy-start.38 = (f32[8,2,32]{2,1,0:T(2,128)S(1)}, f32[8,2,32]{2,1,0:T(2,128)}, u32[]{:S(2)}) copy-start(f32[8,2,32]{2,1,0:T(2,128)} %get-tuple-element.61) | copy-start | bytes 6148
  148.2 4.3 %copy-start.37 = (f32[8,2,32]{2,1,0:T(2,128)S(1)}, f32[8,2,32]{2,1,0:T(2,128)}, u32[]{:S(2)}) copy-start(f32[8,2,32]{2,1,0:T(2,128)} %get-tuple-element.62) | copy-start | bytes 6148
  148.2 5.2 %copy-start.36 = (f32[8,1,1,2]{1,2,3,0:T(1,128)S(1)}, f32[8,1,1,2]{1,2,3,0:T(1,128)}, u32[]{:S(2)}) copy-start(f32[8,1,1,2]{1,2,3,0:T(1,128)} %get-tuple-element.66) | copy-start | bytes 196
  148.2 5.4 %copy-start.35 = (f32[8,1,1,2]{1,2,3,0:T(1,128)S(1)}, f32[8,1,1,2]{1,2,3,0:T(1,128)}, u32[]{:S(2)}) copy-start(f32[8,1,1,2]{1,2,3,0:T(1,128)} %get-tuple-element.65) | copy-start | bytes 196
  148.2 5.6 %copy-start.34 = (f32[8,1,1,2]{1,2,3,0:T(1,128)S(1)}, f32[8,1,1,2]{1,2,3,0:T(1,128)}, u32[]{:S(2)}) copy-start(f32[8,1,1,2]{1,2,3,0:T(1,128)} %get-tuple-element.64) | copy-start | bytes 196
  148.2 5.7 %copy-start.27 = (f32[8,4,2,32]{3,2,1,0:T(2,128)S(1)}, f32[8,4,2,32]{3,2,1,0:T(2,128)}, u32[]{:S(2)}) copy-start(f32[8,4,2,32]{3,2,1,0:T(2,128)} %copy-done.26) | copy-start | bytes 24580
  156.7 28.4 %copy-start.1 = (f32[2,2,32,32,128]{4,3,2,1,0:T(8,128)S(1)}, f32[2,2,32,32,128]{4,3,2,1,0:T(8,128)}, u32[]{:S(2)}) copy-start(f32[2,2,32,32,128]{4,3,2,1,0:T(8,128)} %get-tuple-element.15) | copy-start | bytes 6291460
  188.1 65.4 %collective-permute-start.2 = (bf16[2,2,32,32,128]{4,3,2,1,0:T(8,128)(2,1)}, bf16[2,2,32,32,128]{4,3,2,1,0:T(8,128)(2,1)}, u32[]{:S(2)}, u32[]{:S(2)}) collective-permute-start(bf16[2,2,32,32,128]{4,3,2,1,0:T(8,128)(2,1)} %fusion.30), channel_id=1, source_target_pairs={{0,8},{4,12},{2,10},{6,14},{1,9},{5,13},{3,11},{7,15},{16,24},{20,... | collective-permute-start | bytes 3145736 | tf_op jit(solution)/shard_map/ppermute | solution.py:73
  253.4 10.7 %copy-start.13 = (f32[8,1,4096]{2,0,1:T(8,128)S(1)}, f32[8,1,4096]{2,0,1:T(8,128)}, u32[]{:S(2)}) copy-start(f32[8,1,4096]{2,0,1:T(8,128)} %squeeze.40) | copy-start | bytes 393220
  253.4 10.7 %copy-start.15 = (f32[8,1,4096]{2,0,1:T(8,128)S(1)}, f32[8,1,4096]{2,0,1:T(8,128)}, u32[]{:S(2)}) copy-start(f32[8,1,4096]{2,0,1:T(8,128)} %mul.677) | copy-start | bytes 393220
  253.5 10.7 %copy-start.16 = (f32[8,1,4096]{2,0,1:T(8,128)S(1)}, f32[8,1,4096]{2,0,1:T(8,128)}, u32[]{:S(2)}) copy-start(f32[8,1,4096]{2,0,1:T(8,128)} %mul.693) | copy-start | bytes 393220
  253.5 10.7 %copy-start.17 = (f32[8,1,4096]{2,0,1:T(8,128)S(1)}, f32[8,1,4096]{2,0,1:T(8,128)}, u32[]{:S(2)}) copy-start(f32[8,1,4096]{2,0,1:T(8,128)} %mul.699) | copy-start | bytes 393220
  253.5 10.7 %copy-start.18 = (f32[8,1,4096]{2,0,1:T(8,128)S(1)}, f32[8,1,4096]{2,0,1:T(8,128)}, u32[]{:S(2)}) copy-start(f32[8,1,4096]{2,0,1:T(8,128)} %mul.669) | copy-start | bytes 393220
  253.5 10.7 %copy-start.19 = (f32[8,1,4096]{2,0,1:T(8,128)S(1)}, f32[8,1,4096]{2,0,1:T(8,128)}, u32[]{:S(2)}) copy-start(f32[8,1,4096]{2,0,1:T(8,128)} %mul.687) | copy-start | bytes 393220
  253.5 10.7 %copy-start.20 = (f32[8,1,4096]{2,0,1:T(8,128)S(1)}, f32[8,1,4096]{2,0,1:T(8,128)}, u32[]{:S(2)}) copy-start(f32[8,1,4096]{2,0,1:T(8,128)} %squeeze.38) | copy-start | bytes 393220
  253.5 10.7 %copy-start.21 = (f32[8,1,4096]{2,0,1:T(8,128)S(1)}, f32[8,1,4096]{2,0,1:T(8,128)}, u32[]{:S(2)}) copy-start(f32[8,1,4096]{2,0,1:T(8,128)} %squeeze.41) | copy-start | bytes 393220
  253.5 10.7 %copy-start.22 = (f32[8,1,4096]{2,0,1:T(8,128)S(1)}, f32[8,1,4096]{2,0,1:T(8,128)}, u32[]{:S(2)}) copy-start(f32[8,1,4096]{2,0,1:T(8,128)} %squeeze.36) | copy-start | bytes 393220
  253.5 10.7 %copy-start.23 = (f32[8,1,4096]{2,0,1:T(8,128)S(1)}, f32[8,1,4096]{2,0,1:T(8,128)}, u32[]{:S(2)}) copy-start(f32[8,1,4096]{2,0,1:T(8,128)} %squeeze.39) | copy-start | bytes 393220
  256.6 25.4 %collective-permute-start.3 = (bf16[2,2,32,32,128]{4,3,2,1,0:T(8,128)(2,1)}, bf16[2,2,32,32,128]{4,3,2,1,0:T(8,128)(2,1)}, u32[]{:S(2)}, u32[]{:S(2)}) collective-permute-start(bf16[2,2,32,32,128]{4,3,2,1,0:T(8,128)(2,1)} %select_convert_fusion), channel_id=1, source_target_pairs={{0,2},{4,6},{8,10},{12,14},{2,0},{6,4},{10,8},{14,12},{1,3},{5,7},... | collective-permute-start | bytes 3145736 | tf_op jit(solution)/shard_map/ppermute | solution.py:73
  264.3 17.7 %copy-start.43 = (f32[2,2,32]{2,1,0:T(2,128)S(1)}, f32[2,2,32]{2,1,0:T(2,128)}, u32[]{:S(2)}) copy-start(f32[2,2,32]{2,1,0:T(2,128)} %exp.222) | copy-start | bytes 1540
  264.4 17.7 %copy-start.45 = (f32[2,2,32]{2,1,0:T(2,128)S(1)}, f32[2,2,32]{2,1,0:T(2,128)}, u32[]{:S(2)}) copy-start(f32[2,2,32]{2,1,0:T(2,128)} %exp.230) | copy-start | bytes 1540
  264.4 17.7 %copy-start.47 = (f32[2,2,32]{2,1,0:T(2,128)S(1)}, f32[2,2,32]{2,1,0:T(2,128)}, u32[]{:S(2)}) copy-start(f32[2,2,32]{2,1,0:T(2,128)} %exp.232) | copy-start | bytes 1540
  275.1 9.8 %copy-start.2 = (bf16[1,256,4096]{1,2,0:T(8,128)(2,1)S(1)}, bf16[1,256,4096]{1,2,0:T(8,128)(2,1)}, u32[]{:S(2)}) copy-start(bf16[1,256,4096]{1,2,0:T(8,128)(2,1)} %copy.105) | copy-start | bytes 6291460
  275.1 9.8 %copy-start.29 = (f32[64,256]{1,0:T(8,128)S(1)}, f32[64,256]{1,0:T(8,128)}, u32[]{:S(2)}) copy-start(f32[64,256]{1,0:T(8,128)} %get-tuple-element.51) | copy-start | bytes 196612
  275.1 9.8 %copy-start.49 = (f32[2,32]{1,0:T(2,128)S(1)}, f32[2,32]{1,0:T(2,128)}, u32[]{:S(2)}) copy-start(f32[2,32]{1,0:T(2,128)} %copy-done.48) | copy-start | bytes 772
  284.9 4.2 %copy-start.6 = (f32[2,2,32,32,128]{4,3,2,1,0:T(8,128)}, f32[2,2,32,32,128]{4,3,2,1,0:T(8,128)S(1)}, u32[]{:S(2)}) copy-start(f32[2,2,32,32,128]{4,3,2,1,0:T(8,128)S(1)} %get-tuple-element.16) | copy-start | bytes 6291460
  284.9 4.2 %copy-start.7 = (f32[2,2,32,32,128]{4,3,2,1,0:T(8,128)}, f32[2,2,32,32,128]{4,3,2,1,0:T(8,128)S(1)}, u32[]{:S(2)}) copy-start(f32[2,2,32,32,128]{4,3,2,1,0:T(8,128)S(1)} %get-tuple-element.17) | copy-start | bytes 6291460
  289.1 4.4 %copy-start.5 = (bf16[1,256,4096]{1,2,0:T(8,128)(2,1)S(1)}, bf16[1,256,4096]{1,2,0:T(8,128)(2,1)}, u32[]{:S(2)}) copy-start(bf16[1,256,4096]{1,2,0:T(8,128)(2,1)} %copy.110) | copy-start | bytes 6291460
  289.2 4.4 %copy-start.28 = (f32[64,256]{1,0:T(8,128)S(1)}, f32[64,256]{1,0:T(8,128)}, u32[]{:S(2)}) copy-start(f32[64,256]{1,0:T(8,128)} %get-tuple-element.50) | copy-start | bytes 196612
  300.1 4.3 %copy-start.10 = (bf16[1,256,4096]{2,1,0:T(8,128)(2,1)S(1)}, bf16[1,256,4096]{2,1,0:T(8,128)(2,1)}, u32[]{:S(2)}) copy-start(bf16[1,256,4096]{2,1,0:T(8,128)(2,1)} %copy.119) | copy-start | bytes 6291460
  (9 other events, 16.8 us)
Sparse Core Ops, SparseCore 0:
  18.8 73.6 all-reduce.6
  132.2 110.3 all-reduce.4
where the time goes:
time: 317 us; the launch traced here: 315 us
  local copies, waits for them, and re-layouts  109 us (34%)
  waiting for transfers between devices  90.2 us (28%)
  matrix products  52.7 us (17%)
  other arithmetic  31.6 us (10%)
  between operations  16.2 us (5%)
  starting transfers between devices  11.6 us (4%)
  blocking collectives  4.36 us (1%)
    psum x1, waiting for transfers between devices, shards(): from_prompt = lax.psum(contribution, 'ctx')  53.2 us
    unnamed x3, waiting for transfers between devices  30 us
    mul x20, local copies, waits for them, and re-layouts, shards(): value = value + coefficient[..., None] * driven[:, v]  15.8 us
    dot_general x2, matrix products, block_terms(): jnp.einsum('gkts,sgkp->tgkp', mixing, inputs_head, preferred_element_type...  14.6 us
    dot_general x1, matrix products, shards(): jnp.einsum('rgkpn,jugn->rjugkp', weighted_states, all_c, precision=HIGH)  12.9 us
    convert_element_type x4, other arithmetic, send(): value.astype(jnp.bfloat16)  11.5 us
    ppermute x4, starting transfers between devices, send(): lax.ppermute(value.astype(jnp.bfloat16), 'ctx', pairs).astype(jnp.float32)  11.5 us
    slice x3, local copies, waits for them, and re-layouts, shards(): ssm_input[request]  10.6 us
  transfers between devices with their start and end apart: 6, of which 3 were waited for; matrix products, arithmetic and copies ran while one was open for 48% of the time, Pallas kernels for 0%

commit v1 on v0

--- a/solution.py
+++ b/solution.py
@@ -177,7 +177,8 @@
     request_numbers = lax.broadcasted_iota(jnp.int32, (request_count, 1), 0).astype(jnp.float32)
     chosen = (request_numbers == all_request[None, :]).astype(jnp.float32)
     contribution = jnp.einsum("rj,rjugkp->jugkp", chosen, projected, precision=HIGH)
-    from_prompt = lax.psum(contribution, "ctx")
+    outer = jax.lax.all_gather(contribution, "ctx")
+    from_prompt = jnp.sum(outer, 0)
     cum_logd = jnp.cumsum(all_logd, axis=1)
     inner = jnp.einsum("jvgn,jugn->jvug", all_b, all_c, precision=HIGH)
     driven = all_step[..., None] * all_input

time: 317 us -> 411 us (1.30)
  waiting for transfers between devices: 90.2 us -> 176 us
  local copies, waits for them, and re-layouts: 109 us -> 116 us
  starting transfers between devices: 11.6 us -> 5.57 us
    ppermute x4, waiting for transfers between devices: 6.9 us -> 128 us  [send(): lax.ppermute(value.astype(jnp.bfloat16), 'ctx', pairs).astype(jnp.float32)]
    psum x1 -> x0, waiting for transfers between devices: 53.2 us -> none  [shards(): from_prompt = lax.psum(contribution, 'ctx')]
    unnamed x3, waiting for transfers between devices: 30 us -> 48.1 us
    mul x20, local copies, waits for them, and re-layouts: 15.8 us -> 25.5 us  [shards(): value = value + coefficient[..., None] * driven[:, v]]
    ppermute x4, starting transfers between devices: 11.5 us -> 5.49 us  [send(): lax.ppermute(value.astype(jnp.bfloat16), 'ctx', pairs).astype(jnp.float32)]
    exp x12, local copies, waits for them, and re-layouts: 9.99 us -> 4.22 us  [range_decay(): return jnp.exp(jnp.sum(jnp.where(keep, all_totals, 0.0), axis=0))]
    squeeze x4, local copies, waits for them, and re-layouts: 6.87 us -> 1.78 us  [shards(): value = jnp.exp(cum_logd[:, u])[..., None] * from_prompt[:, u]]
    reduce_sum x0 -> x1, other arithmetic: none -> 4.58 us  [shards(): from_prompt = jnp.sum(outer, 0)]
  transfers between devices with their start and end apart: 6 -> 6, of which waited for: 3 -> 3; matrix products, arithmetic and copies ran while one was open for 48% -> 44% of each run, Pallas kernels for 0% -> 0%
where the time goes in v1:
time: 411 us; the launch traced here: 408 us
  waiting for transfers between devices  176 us (43%)
  local copies, waits for them, and re-layouts  116 us (28%)
  matrix products  54.9 us (13%)
  other arithmetic  35.5 us (9%)
  between operations  16.4 us (4%)
  starting transfers between devices  5.57 us (1%)
    ppermute x4, waiting for transfers between devices, send(): lax.ppermute(value.astype(jnp.bfloat16), 'ctx', pairs).astype(jnp.float32)  128 us
    unnamed x3, waiting for transfers between devices  48.1 us
    mul x20, local copies, waits for them, and re-layouts, shards(): value = value + coefficient[..., None] * driven[:, v]  25.5 us
    dot_general x2, matrix products, block_terms(): jnp.einsum('gkts,sgkp->tgkp', mixing, inputs_head, preferred_element_type...  14.4 us
    unnamed x141, local copies, waits for them, and re-layouts  13.8 us
    dot_general x1, matrix products, shards(): jnp.einsum('rgkpn,jugn->rjugkp', weighted_states, all_c, precision=HIGH)  12.9 us
    convert_element_type x4, other arithmetic, send(): value.astype(jnp.bfloat16)  11.4 us
    dot_general x2, matrix products, finish(): carried = jnp.einsum('tgn,gkpn->tgkp', c_groups, entering, precision=HIGH)  10.6 us
  transfers between devices with their start and end apart: 6, of which 3 were waited for; matrix products, arithmetic and copies ran while one was open for 44% of the time, Pallas kernels for 0%

profile of v1, /device:TPU:26, one launch (start us, length us, event | category | flops | bytes accessed | tf_op | source)
XLA Modules:
  0.0 408.5 jit_solution(5696635481940201439)
XLA Ops:
  19.5 3.9 fusion.76
  23.4 4.1 %copy.211 = bf16[1,256,4096]{1,2,0:T(8,128)(2,1)} copy(bf16[1,256,4096]{2,1,0:T(8,128)(2,1)} %get-tuple-element.22) | data formatting | bytes 4194304 | tf_op jit(solution)/shard_map/slice | solution.py:138
  27.7 2.5 copy.216
  30.3 2.5 fusion.52
  44.5 48.0 %all-reduce.4.cloned.1.call-done = f32[152584]{0:T(1024)} async-done(((f32[152584]{0:T(1024)}), f32[152584]{0:T(1024)}) %all-reduce.4.cloned.1.call-update) | async-done | bytes 610352
  92.5 2.3 reshape.861
  98.8 12.9 %fusion.49 = f32[2,8,4,2,32,64]{5,1,4,0,2,3:T(8,128)S(1)} fusion(f32[8,4,2,128,1,1]{3,0,2,1,5,4:T(8,128)S(1)} %bitcast.254, f32[1,2,32,64,128]{4,3,2,1,0:T(8,128)} %copy-done, f32[1,2,32,64,128]{4,3,2,1,0:T(8,128)S(1)} %fusion.52, f32[2,2,32]{2,1,0:T(2,128)S(1)} %exp.239), kind=kOutput, calls=%fused_computation.71 | convolution fusion | flops 404750336 | bytes 5276160 | tf_op jit(solution)/shard_map/rgkpn,jugn->rjugkp/dot_general | solution.py:176
  111.7 5.7 %fusion.47 = f32[8,1,4,2,32,64]{5,1,4,3,2,0:T(1,128)} fusion(pred[2,8,1,1,1,1]{0,2,5,4,3,1:T(4,128)(4,1)S(1)} %copy.268, f32[2,8,4,2,32,64]{5,1,4,0,2,3:T(8,128)S(1)} %fusion.49), kind=kOutput, calls=%fused_computation.69 | convolution fusion | flops 3145728 | bytes 1572880 | tf_op jit(solution)/shard_map/rj,rjugkp->jugkp/dot_general | solution.py:179
  117.5 7.9 %fusion = f32[2,32,256,64]{2,3,1,0:T(8,128)} fusion(bf16[256,2,32,64]{0,3,2,1:T(8,128)(2,1)} %bitcast.237, f32[2,32,256]{2,1,0:T(8,128)} %bitcast.263, f32[2,32,256]{2,1,0:T(8,128)S(1)} %copy-done.42, f32[2,256,256]{2,1,0:T(8,128)} %fusion.88, pred[256,256]{1,0:T(8,128)(4,1)S(1)} %copy-done.40), kind=kOutput, calls=%fused_computation.2 | convolution fusion | flops 562036736 | bytes 7012352 | tf_op jit(solution)/shard_map/gkts,sgkp->tgkp/dot_general | solution.py:34
  128.6 2.0 fusion.89
  132.0 4.0 fusion.58
  137.3 6.5 %fusion.1 = f32[2,32,256,64]{2,3,1,0:T(8,128)} fusion(bf16[256,2,32,64]{0,3,2,1:T(8,128)(2,1)S(1)} %bitcast.240, f32[2,32,256]{2,1,0:T(8,128)S(1)} %bitcast.262, f32[2,32,256]{2,1,0:T(8,128)S(1)} %copy-done.43, f32[2,256,256]{2,1,0:T(8,128)S(1)} %copy-done.35, pred[256,256]{1,0:T(8,128)(4,1)S(1)} %copy-done.41), kind=kOutput, calls=%fused_computation.3 | convolution fusion | flops 562036736 | bytes 7012352 | tf_op jit(solution)/shard_map/gkts,sgkp->tgkp/dot_general | solution.py:34
  143.9 41.0 %collective-permute-done.1 = bf16[2,2,32,32,128]{4,3,2,1,0:T(8,128)(2,1)} collective-permute-done((bf16[2,2,32,32,128]{4,3,2,1,0:T(8,128)(2,1)}, bf16[2,2,32,32,128]{4,3,2,1,0:T(8,128)(2,1)}, u32[]{:S(2)}, u32[]{:S(2)}) %collective-permute-start.1) | collective-permute-done | bytes 1048608 | tf_op jit(solution)/shard_map/ppermute | solution.py:73
  184.9 2.9 fusion.30
  196.8 2.5 reshape_reshape.15
  202.1 2.6 broadcast_multiply_fusion
  204.7 87.2 %collective-permute-done.2 = bf16[2,2,32,32,128]{4,3,2,1,0:T(8,128)(2,1)} collective-permute-done((bf16[2,2,32,32,128]{4,3,2,1,0:T(8,128)(2,1)}, bf16[2,2,32,32,128]{4,3,2,1,0:T(8,128)(2,1)}, u32[]{:S(2)}, u32[]{:S(2)}) %collective-permute-start.2) | collective-permute-done | bytes 1048608 | tf_op jit(solution)/shard_map/ppermute | solution.py:73
  292.0 2.9 select_convert_fusion
  297.4 1.7 mul.677
  300.0 1.7 mul.693
  302.6 1.7 mul.699
  304.3 2.3 fusion.79
  306.6 1.7 squeeze.37
  310.9 1.7 mul.669
  315.2 2.1 fusion.78
  318.0 1.7 squeeze.38
  321.4 1.7 squeeze.41
  326.4 1.7 mul.715
  329.0 1.7 mul.721
  331.5 1.7 mul.731
  334.7 1.7 mul.737
  337.3 1.7 mul.743
  339.8 1.7 mul.749
  341.5 1.7 squeeze.43
  343.3 1.7 squeeze.46
  345.8 1.7 mul.703
  348.4 1.7 mul.725
  351.7 1.7 squeeze.44
  355.1 1.7 squeeze.47
  356.9 2.6 convert_select_fusion.1
  361.0 4.0 fusion.18
  365.0 4.3 %copy.225 = bf16[1,256,4096]{2,1,0:T(8,128)(2,1)} copy(bf16[1,256,4096]{1,2,0:T(8,128)(2,1)} %bitcast.243) | data formatting | bytes 4194304 | tf_op jit(solution)/shard_map/convert_element_type | solution.py:58
  369.3 6.6 %fusion.21 = bf16[256,2,32,64]{0,3,2,1:T(8,128)(2,1)} fusion(bf16[256,2,32,64]{0,3,2,1:T(8,128)(2,1)S(1)} %bitcast.241, f32[2,32,256,64]{2,3,1,0:T(8,128)} %fusion.1, bf16[256,2,128,1]{0,2,3,1:T(8,128)(2,1)S(1)} %bitcast.248, f32[2,2,32,32,128]{4,3,2,1,0:T(8,128)} %copy-done.7, f32[2,2,32,32,128]{4,3,2,1,0:T(8,128)} %copy-done.6, ...), kind=kOutput, calls=%fused_computation.32 | convolution fusion | flops 1617428480 | bytes 12779776 | tf_op jit(solution)/shard_map/tgn,gkpn->tgkp/dot_general | solution.py:51
  375.9 4.3 %copy.226 = bf16[1,256,4096]{2,1,0:T(8,128)(2,1)} copy(bf16[1,256,4096]{1,2,0:T(8,128)(2,1)} %bitcast.242) | data formatting | bytes 4194304 | tf_op jit(solution)/shard_map/convert_element_type | solution.py:58
  380.2 4.0 pad_maximum_fusion.1
  384.2 4.6 %reduce_sum.69 = f32[8,4,2,32,64]{4,3,2,1,0:T(8,128)S(1)} reduce(f32[8,8,4,2,32,64]{5,4,3,2,1,0:T(8,128)} %bitcast.244, f32[]{:T(128)} %constant.38.clone.1), dimensions={0}, to_apply=%region_11.12 | reduce | flops 917504 | bytes 4718596 | tf_op jit(solution)/shard_map/reduce_sum | solution.py:181
  392.2 4.9 %fusion.2 = f32[8,4,1024]{2,0,1:T(8,128)S(1)} fusion(bf16[4096,1024]{1,0:T(8,128)(2,1)} %param.25, bf16[8,1,4096]{2,0,1:T(8,128)(2,1)S(1)} %get-tuple-element.41, bf16[8,1,4096]{2,0,1:T(8,128)(2,1)S(1)} %get-tuple-element.40, bf16[8,1,4096]{2,0,1:T(8,128)(2,1)S(1)} %get-tuple-element.47, bf16[8,1,4096]{2,0,1:T(8,128)(2,1)S(1)} %get-tuple-element.46), kind=kOutput, calls=%fused_computation.4 | convolution fusion | flops 268828672 | bytes 8781824 | tf_op jit(solution)/shard_map/jup,pd->jud/dot_general | solution.py:195
  397.1 3.8 all-reduce.5
  (270 shorter events, 74.6 us)
Async XLA Ops:
  7.2 11.5 %copy-start.36 = (f32[2,64,256]{2,1,0:T(8,128)S(1)}, f32[2,64,256]{2,1,0:T(8,128)}, u32[]{:S(2)}) copy-start(f32[2,64,256]{2,1,0:T(8,128)} %param.16) | copy-start | bytes 393220
  7.2 85.4 %all-reduce.4.cloned.1.call-start = ((), (), s32[]{:S(2)}) async-start(), calls=%async_computation.1 | async-start | bytes 1228800
  9.0 14.4 %copy-start.51 = (f32[64,2]{0,1:T(2,128)}, f32[64,2]{0,1:T(2,128)S(1)}, u32[]{:S(2)}) copy-start(f32[64,2]{0,1:T(2,128)S(1)} %slice.199) | copy-start | bytes 1540
  18.6 365.6 %all-gather.4.cloned.1.call-start = ((), (), s32[]{:S(2)}) async-start(), calls=%async_computation | async-start | bytes 9437184 | tf_op jit(solution)/shard_map/all_gather | solution.py:180
  23.4 4.2 %copy-start.39 = (bf16[2,256,256]{2,1,0:T(8,128)(2,1)S(1)}, bf16[2,256,256]{2,1,0:T(8,128)(2,1)}, u32[]{:S(2)}) copy-start(bf16[2,256,256]{2,1,0:T(8,128)(2,1)} %param.14) | copy-start | bytes 786436
  35.2 96.7 %collective-permute-start = (bf16[2,2,32,32,128]{4,3,2,1,0:T(8,128)(2,1)}, bf16[2,2,32,32,128]{4,3,2,1,0:T(8,128)(2,1)S(1)}, u32[]{:S(2)}, u32[]{:S(2)}) collective-permute-start(bf16[2,2,32,32,128]{4,3,2,1,0:T(8,128)(2,1)} %select_convert_fusion.1), channel_id=1, source_target_pairs={{0,2},{4,6},{8,10},{12,14},{2,0},{6,4},{10,8},{14,12},{1,3},{5,7},... | collective-permute-start | bytes 3145736 | tf_op jit(solution)/shard_map/ppermute | solution.py:73
  111.7 5.7 %copy-start.40 = (pred[256,256]{1,0:T(8,128)(4,1)S(1)}, pred[256,256]{1,0:T(8,128)(4,1)}, u32[]{:S(2)}) copy-start(pred[256,256]{1,0:T(8,128)(4,1)} %iota_compare_fusion) | copy-start | bytes 196612
  111.7 5.7 %copy-start.42 = (f32[2,32,256]{2,1,0:T(8,128)S(1)}, f32[2,32,256]{2,1,0:T(8,128)}, u32[]{:S(2)}) copy-start(f32[2,32,256]{2,1,0:T(8,128)} %reduce_window_sum.59) | copy-start | bytes 196612
  117.5 7.9 %copy-start.62 = (f32[64]{0:T(128)S(1)}, f32[64]{0:T(128)}, u32[]{:S(2)}) copy-start(f32[64]{0:T(128)} %param.18) | copy-start | bytes 772
  131.9 5.3 %copy-start.4 = (bf16[1,256,4096]{1,2,0:T(8,128)(2,1)S(1)}, bf16[1,256,4096]{1,2,0:T(8,128)(2,1)}, u32[]{:S(2)}) copy-start(bf16[1,256,4096]{1,2,0:T(8,128)(2,1)} %copy.216) | copy-start | bytes 6291460
  131.9 5.3 %copy-start.35 = (f32[2,256,256]{2,1,0:T(8,128)S(1)}, f32[2,256,256]{2,1,0:T(8,128)}, u32[]{:S(2)}) copy-start(f32[2,256,256]{2,1,0:T(8,128)} %fusion.89) | copy-start | bytes 1572868
  131.9 5.3 %copy-start.41 = (pred[256,256]{1,0:T(8,128)(4,1)S(1)}, pred[256,256]{1,0:T(8,128)(4,1)}, u32[]{:S(2)}) copy-start(pred[256,256]{1,0:T(8,128)(4,1)} %iota_compare_fusion) | copy-start | bytes 196612
  131.9 5.3 %copy-start.43 = (f32[2,32,256]{2,1,0:T(8,128)S(1)}, f32[2,32,256]{2,1,0:T(8,128)}, u32[]{:S(2)}) copy-start(f32[2,32,256]{2,1,0:T(8,128)} %reduce_window_sum.63) | copy-start | bytes 196612
  131.9 5.3 %copy-start.44 = (f32[1,64,256]{2,1,0:T(8,128)S(1)}, f32[1,64,256]{2,1,0:T(8,128)}, u32[]{:S(2)}) copy-start(f32[1,64,256]{2,1,0:T(8,128)} %get-tuple-element.49) | copy-start | bytes 196612
  135.9 48.9 %collective-permute-start.1 = (bf16[2,2,32,32,128]{4,3,2,1,0:T(8,128)(2,1)}, bf16[2,2,32,32,128]{4,3,2,1,0:T(8,128)(2,1)}, u32[]{:S(2)}, u32[]{:S(2)}) collective-permute-start(bf16[2,2,32,32,128]{4,3,2,1,0:T(8,128)(2,1)} %get-tuple-element.18), channel_id=1, source_target_pairs={{0,4},{4,8},{8,12},{2,6},{6,10},{10,14},{1,5},{5,9},{9,13},{3,7},{... | collective-permute-start | bytes 3145736 | tf_op jit(solution)/shard_map/ppermute | solution.py:73
  137.3 6.5 %copy-start.61 = (f32[128]{0:T(128)S(1)}, f32[128]{0:T(128)}, u32[]{:S(2)}) copy-start(f32[128]{0:T(128)} %get-tuple-element.13) | copy-start | bytes 1540
  137.3 47.6 %copy-start.1 = (f32[2,2,32,32,128]{4,3,2,1,0:T(8,128)S(1)}, f32[2,2,32,32,128]{4,3,2,1,0:T(8,128)}, u32[]{:S(2)}) copy-start(f32[2,2,32,32,128]{4,3,2,1,0:T(8,128)} %get-tuple-element.19) | copy-start | bytes 6291460
  184.9 4.5 %copy-start.10 = (f32[8,19073]{1,0:T(8,128)S(1)}, f32[8,19073]{1,0:T(8,128)}, u32[]{:S(2)}) copy-start(f32[8,19073]{1,0:T(8,128)} %reshape.861) | copy-start | bytes 1831012
  187.8 104.2 %collective-permute-start.2 = (bf16[2,2,32,32,128]{4,3,2,1,0:T(8,128)(2,1)}, bf16[2,2,32,32,128]{4,3,2,1,0:T(8,128)(2,1)}, u32[]{:S(2)}, u32[]{:S(2)}) collective-permute-start(bf16[2,2,32,32,128]{4,3,2,1,0:T(8,128)(2,1)} %fusion.30), channel_id=1, source_target_pairs={{0,8},{4,12},{2,10},{6,14},{1,9},{5,13},{3,11},{7,15},{16,24},{20,... | collective-permute-start | bytes 3145736 | tf_op jit(solution)/shard_map/ppermute | solution.py:73
  200.1 94.7 %copy-start.45 = (f32[2,2,32]{2,1,0:T(2,128)}, f32[2,2,32]{2,1,0:T(2,128)S(1)}, u32[]{:S(2)}) copy-start(f32[2,2,32]{2,1,0:T(2,128)S(1)} %exp.222) | copy-start | bytes 1540
  200.9 94.0 %copy-start.47 = (f32[2,2,32]{2,1,0:T(2,128)}, f32[2,2,32]{2,1,0:T(2,128)S(1)}, u32[]{:S(2)}) copy-start(f32[2,2,32]{2,1,0:T(2,128)S(1)} %exp.230) | copy-start | bytes 1540
  202.1 89.9 %copy-start.49 = (f32[2,2,32]{2,1,0:T(2,128)S(1)}, f32[2,2,32]{2,1,0:T(2,128)}, u32[]{:S(2)}) copy-start(f32[2,2,32]{2,1,0:T(2,128)} %exp.232) | copy-start | bytes 1540
  204.7 91.7 %copy-start.52 = (f32[8,2]{1,0:T(8,128)S(1)}, f32[8,2]{1,0:T(8,128)}, u32[]{:S(2)}) copy-start(f32[8,2]{1,0:T(8,128)} %copy.232) | copy-start | bytes 196
  204.7 91.7 %copy-start.53 = (f32[8,2]{1,0:T(8,128)S(1)}, f32[8,2]{1,0:T(8,128)}, u32[]{:S(2)}) copy-start(f32[8,2]{1,0:T(8,128)} %copy.237) | copy-start | bytes 196
  204.7 91.7 %copy-start.54 = (f32[8,2]{1,0:T(8,128)S(1)}, f32[8,2]{1,0:T(8,128)}, u32[]{:S(2)}) copy-start(f32[8,2]{1,0:T(8,128)} %copy.239) | copy-start | bytes 196
  204.7 91.7 %copy-start.55 = (f32[8,2]{1,0:T(8,128)S(1)}, f32[8,2]{1,0:T(8,128)}, u32[]{:S(2)}) copy-start(f32[8,2]{1,0:T(8,128)} %copy.242) | copy-start | bytes 196
  204.7 91.7 %copy-start.56 = (f32[8,2]{1,0:T(8,128)S(1)}, f32[8,2]{1,0:T(8,128)}, u32[]{:S(2)}) copy-start(f32[8,2]{1,0:T(8,128)} %copy.244) | copy-start | bytes 196
  204.7 91.7 %copy-start.57 = (f32[8,2]{1,0:T(8,128)S(1)}, f32[8,2]{1,0:T(8,128)}, u32[]{:S(2)}) copy-start(f32[8,2]{1,0:T(8,128)} %copy.246) | copy-start | bytes 196
  204.7 91.7 %copy-start.58 = (f32[8,2]{1,0:T(8,128)S(1)}, f32[8,2]{1,0:T(8,128)}, u32[]{:S(2)}) copy-start(f32[8,2]{1,0:T(8,128)} %copy.249) | copy-start | bytes 196
  294.9 62.0 %collective-permute-start.3 = (bf16[2,2,32,32,128]{4,3,2,1,0:T(8,128)(2,1)}, bf16[2,2,32,32,128]{4,3,2,1,0:T(8,128)(2,1)}, u32[]{:S(2)}, u32[]{:S(2)}) collective-permute-start(bf16[2,2,32,32,128]{4,3,2,1,0:T(8,128)(2,1)} %select_convert_fusion), channel_id=1, source_target_pairs={{0,2},{4,6},{8,10},{12,14},{2,0},{6,4},{10,8},{14,12},{1,3},{5,7},... | collective-permute-start | bytes 3145736 | tf_op jit(solution)/shard_map/ppermute | solution.py:73
  339.8 17.1 %copy-start.46 = (f32[2,2,32]{2,1,0:T(2,128)S(1)}, f32[2,2,32]{2,1,0:T(2,128)}, u32[]{:S(2)}) copy-start(f32[2,2,32]{2,1,0:T(2,128)} %copy-done.45) | copy-start | bytes 1540
  339.8 17.1 %copy-start.48 = (f32[2,2,32]{2,1,0:T(2,128)S(1)}, f32[2,2,32]{2,1,0:T(2,128)}, u32[]{:S(2)}) copy-start(f32[2,2,32]{2,1,0:T(2,128)} %copy-done.47) | copy-start | bytes 1540
  339.8 17.1 %copy-start.50 = (f32[2,2,32]{2,1,0:T(2,128)S(1)}, f32[2,2,32]{2,1,0:T(2,128)}, u32[]{:S(2)}) copy-start(f32[2,2,32]{2,1,0:T(2,128)} %exp.232) | copy-start | bytes 1540
  356.9 4.1 %copy-start.9 = (f32[2,32,256,64]{2,3,1,0:T(8,128)S(1)}, f32[2,32,256,64]{2,3,1,0:T(8,128)}, u32[]{:S(2)}) copy-start(f32[2,32,256,64]{2,3,1,0:T(8,128)} %fusion) | copy-start | bytes 12582916
  359.5 5.5 %copy-start.6 = (f32[2,2,32,32,128]{4,3,2,1,0:T(8,128)}, f32[2,2,32,32,128]{4,3,2,1,0:T(8,128)S(1)}, u32[]{:S(2)}) copy-start(f32[2,2,32,32,128]{4,3,2,1,0:T(8,128)S(1)} %get-tuple-element.20) | copy-start | bytes 6291460
  359.5 5.5 %copy-start.7 = (f32[2,2,32,32,128]{4,3,2,1,0:T(8,128)}, f32[2,2,32,32,128]{4,3,2,1,0:T(8,128)S(1)}, u32[]{:S(2)}) copy-start(f32[2,2,32,32,128]{4,3,2,1,0:T(8,128)S(1)} %get-tuple-element.21) | copy-start | bytes 6291460
  365.0 4.3 %copy-start.5 = (bf16[1,256,4096]{1,2,0:T(8,128)(2,1)S(1)}, bf16[1,256,4096]{1,2,0:T(8,128)(2,1)}, u32[]{:S(2)}) copy-start(bf16[1,256,4096]{1,2,0:T(8,128)(2,1)} %copy.216) | copy-start | bytes 6291460
  365.0 4.3 %copy-start.37 = (f32[64,256]{1,0:T(8,128)S(1)}, f32[64,256]{1,0:T(8,128)}, u32[]{:S(2)}) copy-start(f32[64,256]{1,0:T(8,128)} %get-tuple-element.54) | copy-start | bytes 196612
  375.9 4.3 %copy-start.8 = (bf16[1,256,4096]{2,1,0:T(8,128)(2,1)S(1)}, bf16[1,256,4096]{2,1,0:T(8,128)(2,1)}, u32[]{:S(2)}) copy-start(bf16[1,256,4096]{2,1,0:T(8,128)(2,1)} %copy.225) | copy-start | bytes 6291460
  389.0 3.0 copy-start.20
  389.0 3.0 copy-start.22
  389.0 3.0 copy-start.24
  389.0 3.0 copy-start.25
  389.0 3.0 copy-start.26
  389.0 3.0 copy-start.27
  389.0 3.0 copy-start.28
  389.0 3.0 copy-start.29
  389.1 3.0 copy-start.30
  (21 other events, 43.9 us)
Sparse Core Ops, SparseCore 0:
  18.7 73.7 all-reduce.3
  117.6 185.2 all-gather.3
